TPU v7x, 32 devices: a whole 2x2x4 slice. The times are simulated.
32 devices in a mesh: narrow: 8 (over z, x), wide: 4 (over y, core).
Axes of the slice: x: 2, y: 2, z: 4, core: 2. Of those that a mesh axis runs over, the one named last changes fastest.
Arguments:
- amps: bfloat16 [16, 512, 512], P(None, 'narrow', 'wide'), may hold values from -1 to 1
- left_fit: bfloat16 [64, 512, 256], P(None, 'narrow'), may hold values from -0.375 to 0.375
- right_fit: bfloat16 [512, 512, 256], P('narrow', 'wide'), may hold values from -0.375 to 0.375
- pair_list: int32 [16, 2], P('narrow'), may hold values from 0 to 127, as said below
- occ_energy: float32 [128], replicated, may hold values from -2 to -0.5
- vir_energy: float32 [512], replicated, may hold values from 0.5 to 3
Outputs:
- update: float32 [16, 64, 512], P('narrow', None, 'wide')
Inputs may be any that keep to these rules, and one draw needn't show every extreme that they name: `pair_list`: each row (i, j) has i <= j.
All inputs are finite; a program needn't handle non-finite values.
Results may differ from a plain program's by a relative error of at most 0.0029.
Values may be sent and summed in bfloat16 or wider, within the bound.
No kernel may reach another device: no remote copies, remote signals or barrier semaphores. Data moves between devices by JAX's collectives and lax.ppermute only.
A program may use at most 128 MiB of HBM per device.

v0:
```python
import jax
import jax.numpy as jnp
from jax import lax
from jax.sharding import PartitionSpec as P

GROUPS = 2


def make_body(n_narrow, n_wide):
    span = n_narrow // GROUPS

    def body(amps, left_fit, right_fit, pair_list, occ_energy, vir_energy):
        n = lax.axis_index("narrow")
        w = lax.axis_index("wide")
        r = n % span
        g = n // span
        b_blk, d_blk, aux = right_fit.shape
        q_blk = aux // span
        rows, c_blk, _ = left_fit.shape
        pairs = amps.shape[0]
        vir_total = b_blk * n_narrow
        amps_all = lax.all_gather(amps, "narrow", axis=1, tiled=True)
        c_sub = c_blk // n_wide
        left_part = lax.dynamic_slice_in_dim(left_fit, w * c_sub, c_sub, 1)
        left_part = left_part.reshape(rows, c_sub, span, q_blk).transpose(2, 0, 1, 3)
        left_send = jnp.concatenate([left_part] * GROUPS, axis=0)
        left_recv = lax.all_to_all(left_send, "narrow", 0, 0, tiled=True)
        left_all = lax.all_gather(left_recv, "wide", axis=0, tiled=False)
        left_all = left_all.transpose(2, 1, 0, 3, 4).reshape(rows, c_blk * n_narrow, q_blk)
        right_split = right_fit.reshape(b_blk, d_blk, span, q_blk)
        chunks = []
        for shift in range(span):
            dest = (r + shift) % span
            piece = lax.dynamic_index_in_dim(right_split, dest, 2, keepdims=False)
            if shift:
                perm = [
                    (gg * span + i, gg * span + (i + shift) % span)
                    for gg in range(GROUPS)
                    for i in range(span)
                ]
                piece = lax.ppermute(piece, "narrow", perm)
            chunks.append(piece)
        inter = jnp.einsum(
            "acq,pcd->padq", left_all, amps_all, preferred_element_type=jnp.float32
        ).astype(jnp.bfloat16)
        right_group = jnp.concatenate(chunks, axis=0)
        part = lax.dot_general(
            inter.reshape(pairs * rows, d_blk * q_blk),
            right_group.reshape(span * b_blk, d_blk * q_blk),
            (((1,), (1,)), ((), ())),
            preferred_element_type=jnp.float32,
        ).reshape(pairs, rows, span, b_blk)
        flipped = jnp.concatenate(
            [part[:, :, (span - k) % span : (span - k) % span + 1] for k in range(span)] * 2, axis=2
        )
        ordered = lax.dynamic_slice_in_dim(flipped, span - r, span, 2)
        ordered = ordered.reshape(pairs, rows, span * b_blk)
        pad = jnp.zeros((pairs, rows, (GROUPS - 1) * span * b_blk), jnp.float32)
        padded = jnp.concatenate([pad, ordered, pad], axis=2)
        ladder = lax.dynamic_slice_in_dim(padded, (GROUPS - 1 - g) * span * b_blk, vir_total, 2)
        ladder = lax.psum_scatter(ladder, "wide", scatter_dimension=2, tiled=True)
        ladder = lax.psum_scatter(ladder, "narrow", scatter_dimension=0, tiled=True)
        local_cols = ladder.shape[2]
        occ_ids = jnp.arange(occ_energy.shape[0], dtype=jnp.int32)
        occ_first = jnp.sum(
            jnp.where(pair_list[:, 0:1] == occ_ids[None, :], occ_energy[None, :], 0.0), axis=1
        )
        occ_second = jnp.sum(
            jnp.where(pair_list[:, 1:2] == occ_ids[None, :], occ_energy[None, :], 0.0), axis=1
        )
        vir_cols = lax.dynamic_slice_in_dim(vir_energy, w * local_cols, local_cols, 0)
        vir_rows = vir_energy[:rows]
        denominator = (
            (occ_first + occ_second)[:, None, None]
            - vir_rows[None, :, None]
            - vir_cols[None, None, :]
        )
        return ladder / denominator

    return body


def solution(mesh):
    return jax.shard_map(
        make_body(mesh.shape["narrow"], mesh.shape["wide"]),
        mesh=mesh,
        in_specs=(
            P(None, "narrow", "wide"),
            P(None, "narrow", None),
            P("narrow", "wide", None),
            P("narrow", None),
            P(),
            P(),
        ),
        out_specs=P("narrow", None, "wide"),
        check_vma=False,
    )
```

profile of v0, /device:TPU:0, one launch (start us, length us, event | category | flops | bytes accessed | tf_op | source)
XLA Modules:
  0.0 375.9 jit_solution(8755748005040324394)
XLA Ops:
  6.5 1.6 copy-done
  8.1 0.8 constant_dynamic-slice_fusion.2
  9.0 2.0 reshape.61
  11.0 1.2 pad_maximum_fusion.1
  12.2 1.7 copy.46
  13.9 3.4 reshape.73
  17.3 32.8 %all_to_all.5 = bf16[8,2,32768]{2,1,0:T(2,128)(2,1)S(1)} all-to-all(bf16[8,2,32768]{2,1,0:T(2,128)(2,1)S(1)} %reshape.73), channel_id=1, replica_groups=mesh['narrow'=8,'wide'=4] {'narrow'}, dimensions={0} | all-to-all | bytes 2097152 | tf_op jit(solution)/shard_map/all_to_all | solution.py:27
  50.1 2.7 reshape.74
  52.8 0.0 all-gather.6.cloned.1.call-update
  52.8 0.0 all-gather.4.cloned.1.call-start
  52.8 0.7 all-gather.4.cloned.1.call-update
  53.5 0.0 reduce-scatter.3.cloned.1.call-start
  53.7 6.4 %copy.50 = bf16[64,128,256]{1,2,0:T(8,128)(2,1)} copy(bf16[64,128,256]{2,1,0:T(8,128)(2,1)} %param.8) | data formatting | bytes 8388608 | tf_op args[2]
  60.1 5.1 %constant_dynamic-slice_fusion.1 = (bf16[64,128,1,64]{1,3,2,0:T(8,128)(2,1)S(1)}, bf16[64,128,64]{1,2,0:T(8,128)(2,1)}, bf16[64,128,64]{1,2,0:T(8,128)(2,1)}, bf16[64,128,64]{1,2,0:T(8,128)(2,1)}) fusion(bf16[64,128,4,64]{1,3,2,0:T(8,128)(2,1)} %bitcast.36, s32[]{:T(128)S(6)} %select_n.62, s32[]{:T(128)S(6)} %select_n.68, s32[]{:T(128)S(6)} %select_n.66, ...), kind=kLoop, calls=%fused_computation.24 | loop fusion | bytes 8388624 | tf_op jit(solution)/shard_map/jit(dynamic_index_in_dim)/dynamic_slice | solution.py:34
  65.2 1.6 collective-permute-start
  66.8 2.6 collective-permute-start.2
  69.4 1.1 copy.51
  70.5 1.7 concatenate.22
  72.2 20.3 %collective-permute-done = bf16[64,128,64]{1,2,0:T(8,128)(2,1)} collective-permute-done((bf16[64,128,64]{1,2,0:T(8,128)(2,1)}, bf16[64,128,64]{1,2,0:T(8,128)(2,1)}, u32[]{:S(2)}, u32[]{:S(2)}) %collective-permute-start) | collective-permute-done | bytes 1048608 | tf_op jit(solution)/shard_map/ppermute | solution.py:41
  92.5 2.0 copy.52
  94.6 2.5 concatenate.23
  97.0 2.0 copy.53
  99.1 2.5 concatenate.24
  101.6 11.2 %collective-permute-done.2 = bf16[64,128,64]{1,2,0:T(8,128)(2,1)} collective-permute-done((bf16[64,128,64]{1,2,0:T(8,128)(2,1)}, bf16[64,128,64]{1,2,0:T(8,128)(2,1)}, u32[]{:S(2)}, u32[]{:S(2)}) %collective-permute-start.2) | collective-permute-done | bytes 1048608 | tf_op jit(solution)/shard_map/ppermute | solution.py:41
  112.7 2.0 copy.54
  114.8 2.5 concatenate.25
  117.3 3.6 pad_maximum_fusion
  120.9 9.1 %copy.47 = bf16[64,8,4,16,64]{4,3,2,1,0:T(8,128)(2,1)} copy(bf16[64,8,4,16,64]{4,3,0,1,2:T(8,128)(2,1)} %bitcast.37) | data formatting | bytes 8388608 | tf_op jit(solution)/shard_map/transpose | solution.py:29
  130.1 31.7 %all-gather.4.cloned.1.call-done = bf16[16,512,128]{2,1,0:T(8,128)(2,1)} async-done(((bf16[16,64,128]{2,1,0:T(8,128)(2,1)}), bf16[16,512,128]{2,1,0:T(8,128)(2,1)}) %all-gather.4.cloned.1.call-update) | async-done | bytes 2097168 | tf_op jit(solution)/shard_map/all_gather | solution.py:22
  161.8 16.0 %convert_bitcast_fusion = bf16[16,64,128,64]{2,3,0,1:T(8,128)(2,1)} fusion(bf16[64,512,64,1]{2,1,3,0:T(8,128)(2,1)} %bitcast.35, bf16[16,512,128]{2,1,0:T(8,128)(2,1)} %all-gather.4.cloned.1.call-done), kind=kOutput, calls=%fused_computation.2 | convolution fusion | flops 8598323200 | bytes 23068672 | tf_op jit(solution)/shard_map/acq,pcd->padq/dot_general | solution.py:43
  177.8 30.3 %copy.49 = bf16[16,64,128,64]{3,2,1,0:T(8,128)(2,1)} copy(bf16[16,64,128,64]{2,3,0,1:T(8,128)(2,1)} %convert_bitcast_fusion) | data formatting | bytes 33554432 | tf_op jit(solution)/shard_map/convert_element_type | solution.py:45
  208.1 44.0 %reshape.68 = bf16[16,64,8192,1]{2,1,0,3:T(8,128)(2,1)} reshape(bf16[16,64,128,64]{3,2,1,0:T(8,128)(2,1)} %copy.49) | data formatting | bytes 33554432 | tf_op jit(solution)/shard_map/dot_general | solution.py:47
  252.1 12.2 %fusion = f32[16,64,4,64]{3,1,2,0:T(8,128)S(1)} fusion(bf16[4,64,8192,1]{2,1,0,3:T(8,128)(2,1)} %bitcast.39, bf16[16,64,8192,1]{2,1,0,3:T(8,128)(2,1)} %reshape.68), kind=kOutput, calls=%fused_computation | convolution fusion | flops 4294967296 | bytes 22020096 | tf_op jit(solution)/shard_map/dot_general | solution.py:47
  264.7 0.1 constant_dynamic-slice_fusion
  264.8 2.8 copy.55
  267.6 2.6 reshape.64
  270.3 0.1 broadcast_in_dim.26
  270.4 1.7 fusion.3
  272.1 0.0 reduce-scatter.3.cloned.1.call-update
  272.1 0.0 reduce-scatter.5.cloned.1.call-start
  272.2 30.0 %reduce-scatter.3.cloned.1.call-done = f32[16,64,128]{2,1,0:T(8,128)} async-done(((f32[16,64,512]{2,1,0:T(8,128)}), f32[16,64,128]{2,1,0:T(8,128)}) %reduce-scatter.3.cloned.1.call-update) | async-done | bytes 524304 | tf_op jit(solution)/shard_map/reduce_scatter | solution.py:61
  302.2 0.0 reduce-scatter.5.cloned.1.call-update
  302.3 0.1 dynamic_slice.32
  302.3 0.2 slice_reduce_fusion
  302.5 0.2 fusion.6
  302.8 0.1 broadcast_subtract_fusion
  302.8 64.9 %reduce-scatter.5.cloned.1.call-done = f32[2,64,128]{2,1,0:T(8,128)} async-done(((f32[16,64,128]{2,1,0:T(8,128)}), f32[2,64,128]{2,1,0:T(8,128)}) %reduce-scatter.5.cloned.1.call-update) | async-done | bytes 65552 | tf_op jit(solution)/shard_map/reduce_scatter | solution.py:62
  367.8 1.6 subtract_divide_fusion
  (24 shorter events, 0.3 us)
Async XLA Ops:
  6.5 1.6 copy-start
  6.5 114.4 %all-gather.6.cloned.1.call-start = ((), (), s32[]{:S(2)}) async-start(), calls=%async_computation.6 | async-start | bytes 10485760 | tf_op jit(solution)/shard_map/all_gather | solution.py:28
  52.8 109.0 %all-gather.4.cloned.1.call-start = ((), (), s32[]{:S(2)}) async-start(), calls=%async_computation.3 | async-start | bytes 2359296 | tf_op jit(solution)/shard_map/all_gather | solution.py:22
  53.5 248.7 %reduce-scatter.3.cloned.1.call-start = ((), (), s32[]{:S(2)}) async-start(), calls=%async_computation.4 | async-start | bytes 2621440 | tf_op jit(solution)/shard_map/reduce_scatter | solution.py:61
  65.2 27.3 %collective-permute-start = (bf16[64,128,64]{1,2,0:T(8,128)(2,1)}, bf16[64,128,64]{1,2,0:T(8,128)(2,1)}, u32[]{:S(2)}, u32[]{:S(2)}) collective-permute-start(bf16[64,128,64]{1,2,0:T(8,128)(2,1)} %get-tuple-element.12), channel_id=1, source_target_pairs={{0,4},{4,8},{8,12},{12,0},{16,20},{20,24},{24,28},{28,16},{1,5},{5... | collective-permute-start | bytes 3145736 | tf_op jit(solution)/shard_map/ppermute | solution.py:41
  66.8 30.2 %collective-permute-start.1 = (bf16[64,128,64]{1,2,0:T(8,128)(2,1)}, bf16[64,128,64]{1,2,0:T(8,128)(2,1)}, u32[]{:S(2)}, u32[]{:S(2)}) collective-permute-start(bf16[64,128,64]{1,2,0:T(8,128)(2,1)} %get-tuple-element.11), channel_id=1, source_target_pairs={{0,8},{4,12},{8,0},{12,4},{16,24},{20,28},{24,16},{28,20},{1,9},{5... | collective-permute-start | bytes 3145736 | tf_op jit(solution)/shard_map/ppermute | solution.py:41
  66.8 45.9 %collective-permute-start.2 = (bf16[64,128,64]{1,2,0:T(8,128)(2,1)}, bf16[64,128,64]{1,2,0:T(8,128)(2,1)}, u32[]{:S(2)}, u32[]{:S(2)}) collective-permute-start(bf16[64,128,64]{1,2,0:T(8,128)(2,1)} %get-tuple-element.10), channel_id=1, source_target_pairs={{0,12},{4,0},{8,4},{12,8},{16,28},{20,16},{24,20},{28,24},{1,13},{... | collective-permute-start | bytes 3145736 | tf_op jit(solution)/shard_map/ppermute | solution.py:41
  267.6 101.7 %copy-start.1 = (bf16[64,64,256]{2,1,0:T(8,128)(2,1)S(1)}, bf16[64,64,256]{2,1,0:T(8,128)(2,1)}, u32[]{:S(2)}) copy-start(bf16[64,64,256]{2,1,0:T(8,128)(2,1)} %param.7) | copy-start | bytes 6291460
  270.2 32.0 %copy-start.4 = (f32[512]{0:T(512)S(1)}, f32[512]{0:T(512)}, u32[]{:S(2)}) copy-start(f32[512]{0:T(512)} %param.11) | copy-start | bytes 6148
  270.2 32.1 %copy-start.2 = (s32[2,2]{1,0:T(2,128)S(1)}, s32[2,2]{1,0:T(2,128)}, u32[]{:S(2)}) copy-start(s32[2,2]{1,0:T(2,128)} %param.9) | copy-start | bytes 52
  270.2 32.3 %copy-start.3 = (f32[128]{0:T(128)S(1)}, f32[128]{0:T(128)}, u32[]{:S(2)}) copy-start(f32[128]{0:T(128)} %param.10) | copy-start | bytes 1540
  270.2 32.5 %slice-start = ((f32[512]{0:T(512)}), f32[64]{0:T(128)S(1)}, s32[]{:S(2)}) async-start(f32[512]{0:T(512)} %param.11), calls=%async_computation.7 | async-start | bytes 1024 | tf_op jit(solution)/shard_map/slice | solution.py:72
  272.1 95.6 %reduce-scatter.5.cloned.1.call-start = ((), (), s32[]{:S(2)}) async-start(), calls=%async_computation.5 | async-start | bytes 589824 | tf_op jit(solution)/shard_map/reduce_scatter | solution.py:62
Sparse Core Ops, SparseCore 0:
  52.9 57.3 all-gather.5
  112.4 49.2 all-gather.3
  272.2 29.9 reduce-scatter.2
  305.8 61.9 reduce-scatter.4
where the time goes:
time: 378 us; the launch traced here: 376 us
  waiting for transfers between devices  159 us (42%)
  local copies, waits for them, and re-layouts  130 us (34%)
  blocking collectives  32.8 us (9%)
  matrix products  28.2 us (7%)
  between operations  13.5 us (4%)
  other arithmetic  8.46 us (2%)
  starting transfers between devices  4.34 us (1%)
    reduce_scatter x1, waiting for transfers between devices, body(): ladder = lax.psum_scatter(ladder, 'narrow', scatter_dimension=0, tiled=True)  64.9 us
    dot_general x1, local copies, waits for them, and re-layouts, body(): lax.dot_general(inter.reshape(pairs * rows, d_blk * q_blk), right_group.r...  44 us
    all_to_all x1, blocking collectives, body(): left_recv = lax.all_to_all(left_send, 'narrow', 0, 0, tiled=True)  32.8 us
    all_gather x1, waiting for transfers between devices, body(): amps_all = lax.all_gather(amps, 'narrow', axis=1, tiled=True)  31.7 us
    ppermute x3, waiting for transfers between devices, body(): piece = lax.ppermute(piece, 'narrow', perm)  31.5 us
    convert_element_type x1, local copies, waits for them, and re-layouts, body(): inter = jnp.einsum('acq,pcd->padq', left_all, amps_all, preferred_element...  30.3 us
    reduce_scatter x1, waiting for transfers between devices, body(): ladder = lax.psum_scatter(ladder, 'wide', scatter_dimension=2, tiled=True)  30 us
    dot_general x1, matrix products, body(): jnp.einsum('acq,pcd->padq', left_all, amps_all, preferred_element_type=jn...  16 us
  transfers between devices with their start and end apart: 7, of which 5 were waited for; matrix products, arithmetic and copies ran while one was open for 11% of the time, Pallas kernels for 0%

commit v1 on v0

--- a/solution.py
+++ b/solution.py
@@ -1,9 +1,46 @@
+import functools
 import jax
 import jax.numpy as jnp
 from jax import lax
 from jax.sharding import PartitionSpec as P
+from jax.lax import axis_index, axis_size, ppermute
 
 GROUPS = 2
+
+
+def begin_pipes(arr_in, which_dim, message):
+    state_next = arr_in.shape
+    high = arr_in.reshape(
+        *state_next[:which_dim],
+        message,
+        state_next[which_dim] // message,
+        *state_next[which_dim + 1 :]
+    )
+    return jnp.moveaxis(high, which_dim, 0)
+
+
+def shape_islands(q_in, ndim_at):
+    q_in = jnp.moveaxis(q_in, 0, ndim_at)
+    w2 = q_in.shape
+    return q_in.reshape(*w2[:ndim_at], w2[ndim_at] * w2[ndim_at + 1], *w2[ndim_at + 2 :])
+
+
+def _produce_lots_all(t0, axis_tag, u, z_in):
+    t_next = axis_size(axis_tag)
+    e_now = axis_index(axis_tag)
+    tmp, left_arr = (t_next, e_now)
+    even = begin_pipes(t0, u, tmp)
+    fields = [even[left_arr]]
+    for idx in range(1, tmp):
+        x_now = even[left_arr ^ idx]
+        local_part = ppermute(x_now, axis_tag, [(kk, kk ^ idx) for kk in range(tmp)])
+        fields.append(local_part)
+    part_next = jnp.stack(fields, axis=0)
+    even = part_next[left_arr ^ jnp.arange(tmp)]
+    return shape_islands(even, z_in)
+
+
+fit_spot_up = functools.partial(_produce_lots_all, axis_tag="narrow", u=0, z_in=0)
 
 
 def make_body(n_narrow, n_wide):
@@ -24,7 +61,7 @@
         left_part = lax.dynamic_slice_in_dim(left_fit, w * c_sub, c_sub, 1)
         left_part = left_part.reshape(rows, c_sub, span, q_blk).transpose(2, 0, 1, 3)
         left_send = jnp.concatenate([left_part] * GROUPS, axis=0)
-        left_recv = lax.all_to_all(left_send, "narrow", 0, 0, tiled=True)
+        left_recv = fit_spot_up(left_send)
         left_all = lax.all_gather(left_recv, "wide", axis=0, tiled=False)
         left_all = left_all.transpose(2, 1, 0, 3, 4).reshape(rows, c_blk * n_narrow, q_blk)
         right_split = right_fit.reshape(b_blk, d_blk, span, q_blk)

time: 378 us -> 463 us (1.22)
  waiting for transfers between devices: 159 us -> 223 us
  starting transfers between devices: 4.34 us -> 38.7 us
  blocking collectives: 32.8 us -> 0 us
  other arithmetic: 8.46 us -> 35.4 us
  local copies, waits for them, and re-layouts: 130 us -> 123 us
    ppermute x0 -> x7, waiting for transfers between devices: none -> 62.7 us  [_produce_lots_all(): ppermute(x_now, axis_tag, [(kk, kk ^ idx) for kk in range(tmp)])]
    all_to_all x1 -> x0, blocking collectives: 32.8 us -> none  [body(): left_recv = lax.all_to_all(left_send, 'narrow', 0, 0, tiled=True)]
    concatenate x1 -> x2, other arithmetic: 1.22 us -> 28.2 us  [body(): left_send = jnp.concatenate([left_part] * GROUPS, axis=0)]
    ppermute x3, starting transfers between devices: 4.21 us -> 24.5 us  [body(): piece = lax.ppermute(piece, 'narrow', perm)]
    ppermute x0 -> x7, starting transfers between devices: none -> 14 us  [_produce_lots_all(): ppermute(x_now, axis_tag, [(kk, kk ^ idx) for kk in range(tmp)])]
    unnamed x20 -> x25, local copies, waits for them, and re-layouts: 14.3 us -> 9.66 us
  transfers between devices with their start and end apart: 7 -> 14, of which waited for: 5 -> 9; matrix products, arithmetic and copies ran while one was open for 11% -> 10% of each run, Pallas kernels for 0% -> 0%
where the time goes in v1:
time: 463 us; the launch traced here: 461 us
  waiting for transfers between devices  223 us (48%)
  local copies, waits for them, and re-layouts  123 us (27%)
  starting transfers between devices  38.7 us (8%)
  other arithmetic  35.4 us (8%)
  matrix products  28.3 us (6%)
  between operations  13.6 us (3%)
    reduce_scatter x1, waiting for transfers between devices, body(): ladder = lax.psum_scatter(ladder, 'narrow', scatter_dimension=0, tiled=True)  64.9 us
    ppermute x7, waiting for transfers between devices, _produce_lots_all(): ppermute(x_now, axis_tag, [(kk, kk ^ idx) for kk in range(tmp)])  62.7 us
    dot_general x1, local copies, waits for them, and re-layouts, body(): lax.dot_general(inter.reshape(pairs * rows, d_blk * q_blk), right_group.r...  44 us
    all_gather x1, waiting for transfers between devices, body(): amps_all = lax.all_gather(amps, 'narrow', axis=1, tiled=True)  35.1 us
    convert_element_type x1, local copies, waits for them, and re-layouts, body(): inter = jnp.einsum('acq,pcd->padq', left_all, amps_all, preferred_element...  30.3 us
    reduce_scatter x1, waiting for transfers between devices, body(): ladder = lax.psum_scatter(ladder, 'wide', scatter_dimension=2, tiled=True)  30 us
    ppermute x3, waiting for transfers between devices, body(): piece = lax.ppermute(piece, 'narrow', perm)  29 us
    concatenate x2, other arithmetic, body(): left_send = jnp.concatenate([left_part] * GROUPS, axis=0)  28.2 us
  transfers between devices with their start and end apart: 14, of which 9 were waited for; matrix products, arithmetic and copies ran while one was open for 10% of the time, Pallas kernels for 0%

profile of v1, /device:TPU:0, one launch (start us, length us, event | category | flops | bytes accessed | tf_op | source)
XLA Modules:
  0.0 461.1 jit_solution(15180232323310994005)
XLA Ops:
  6.5 1.6 copy-done
  8.2 0.4 reshape.93
  8.6 23.3 %fusion.5 = (bf16[1,64,16,64]{3,0,2,1:T(2,128)(2,1)S(1)}, bf16[1,64,16,64]{3,0,2,1:T(2,128)(2,1)}, bf16[1,64,16,64]{3,0,2,1:T(2,128)(2,1)}, bf16[1,64,16,64]{3,0...) fusion(s32[]{:T(128)S(6)} %select_n.101, ...), kind=kLoop, calls=%fused_computation.30 | loop fusion | flops 1572864 | bytes 1310744 | tf_op jit(solution)/shard_map/concatenate | solution.py:63
  31.9 3.0 collective-permute-start.1
  34.9 4.9 %fusion.7 = (bf16[1,64,16,64]{3,0,2,1:T(2,128)(2,1)S(1)}, bf16[1,64,16,64]{3,0,2,1:T(2,128)(2,1)S(1)}) fusion(s32[]{:T(128)S(6)} %select_n.95, bf16[4,64,16,64]{3,0,2,1:T(4,128)(2,1)S(1)} %bitcast.57, s32[]{:T(128)S(6)} %select_n.94), kind=kLoop, calls=%fused_computation.32 | loop fusion | flops 524288 | bytes 786440 | tf_op jit(solution)/shard_map/concatenate | solution.py:63
  39.8 1.6 collective-permute-start
  41.4 3.0 collective-permute-start.3
  44.4 1.3 collective-permute-start.4
  45.7 7.6 %collective-permute-done = bf16[1,64,16,64]{3,0,2,1:T(2,128)(2,1)S(1)} collective-permute-done((bf16[1,64,16,64]{3,0,2,1:T(2,128)(2,1)S(1)}, bf16[1,64,16,64]{3,0,2,1:T(2,128)(2,1)S(1)}, u32[]{:S(2)}, u32[]{:S(2)}) %collective-permute-start) | collective-permute-done | bytes 131104 | tf_op jit(solution)/shard_map/ppermute | solution.py:36
  53.3 2.5 collective-permute-start.5
  55.8 8.3 %collective-permute-done.1 = bf16[1,64,16,64]{3,0,2,1:T(2,128)(2,1)} collective-permute-done((bf16[1,64,16,64]{3,0,2,1:T(2,128)(2,1)}, bf16[1,64,16,64]{3,0,2,1:T(2,128)(2,1)}, u32[]{:S(2)}, u32[]{:S(2)}) %collective-permute-start.1) | collective-permute-done | bytes 131104 | tf_op jit(solution)/shard_map/ppermute | solution.py:36
  64.1 2.7 collective-permute-start.6
  66.8 1.1 bitcast_dynamic-update-slice_fusion.5
  67.9 7.5 %collective-permute-done.2 = bf16[1,64,16,64]{3,0,2,1:T(2,128)(2,1)S(1)} collective-permute-done((bf16[1,64,16,64]{3,0,2,1:T(2,128)(2,1)}, bf16[1,64,16,64]{3,0,2,1:T(2,128)(2,1)S(1)}, u32[]{:S(2)}, u32[]{:S(2)}) %collective-permute-start.2) | collective-permute-done | bytes 131104 | tf_op jit(solution)/shard_map/ppermute | solution.py:36
  75.6 39.3 %collective-permute-done.4 = bf16[1,64,16,64]{3,0,2,1:T(2,128)(2,1)S(1)} collective-permute-done((bf16[1,64,16,64]{3,0,2,1:T(2,128)(2,1)}, bf16[1,64,16,64]{3,0,2,1:T(2,128)(2,1)S(1)}, u32[]{:S(2)}, u32[]{:S(2)}) %collective-permute-start.4) | collective-permute-done | bytes 131104 | tf_op jit(solution)/shard_map/ppermute | solution.py:36
  115.1 2.2 gather_fusion
  117.3 0.7 all-gather.4.cloned.1.call-update
  118.2 6.4 %copy.99 = bf16[64,128,256]{1,2,0:T(8,128)(2,1)} copy(bf16[64,128,256]{2,1,0:T(8,128)(2,1)} %param.8) | data formatting | bytes 8388608 | tf_op args[2]
  124.6 4.6 constant_dynamic-slice_fusion.1
  129.1 0.2 collective-permute-start.7
  129.4 22.0 %collective-permute-start.8 = (bf16[64,128,64]{1,2,0:T(8,128)(2,1)}, bf16[64,128,64]{1,2,0:T(8,128)(2,1)}, u32[]{:S(2)}, u32[]{:S(2)}) collective-permute-start(bf16[64,128,64]{1,2,0:T(8,128)(2,1)} %get-tuple-element.11), channel_id=1, source_target_pairs={{0,8},{4,12},{8,0},{12,4},{16,24},{20,28},{24,16},{28,20},{1,9},{5... | collective-permute-start | bytes 3145736 | tf_op jit(solution)/shard_map/ppermute | solution.py:78
  151.4 2.2 collective-permute-start.9
  153.6 1.1 copy.100
  154.7 1.7 concatenate.22
  156.4 18.8 %collective-permute-done.7 = bf16[64,128,64]{1,2,0:T(8,128)(2,1)} collective-permute-done((bf16[64,128,64]{1,2,0:T(8,128)(2,1)}, bf16[64,128,64]{1,2,0:T(8,128)(2,1)}, u32[]{:S(2)}, u32[]{:S(2)}) %collective-permute-start.7) | collective-permute-done | bytes 1048608 | tf_op jit(solution)/shard_map/ppermute | solution.py:78
  175.3 2.0 copy.101
  177.3 2.5 concatenate.23
  179.8 2.0 copy.102
  181.8 2.5 concatenate.24
  184.4 10.2 %collective-permute-done.9 = bf16[64,128,64]{1,2,0:T(8,128)(2,1)} collective-permute-done((bf16[64,128,64]{1,2,0:T(8,128)(2,1)}, bf16[64,128,64]{1,2,0:T(8,128)(2,1)}, u32[]{:S(2)}, u32[]{:S(2)}) %collective-permute-start.9) | collective-permute-done | bytes 1048608 | tf_op jit(solution)/shard_map/ppermute | solution.py:78
  194.5 2.0 copy.103
  196.6 2.5 concatenate.25
  199.1 3.6 pad_maximum_fusion
  202.7 9.3 %copy.96 = bf16[64,8,4,16,64]{4,3,2,1,0:T(8,128)(2,1)} copy(bf16[64,8,4,16,64]{4,3,0,1,2:T(8,128)(2,1)} %bitcast.58) | data formatting | bytes 8388608 | tf_op jit(solution)/shard_map/transpose | solution.py:66
  212.0 35.1 %all-gather.4.cloned.1.call-done = bf16[16,512,128]{2,1,0:T(8,128)(2,1)} async-done(((bf16[16,64,128]{2,1,0:T(8,128)(2,1)}), bf16[16,512,128]{2,1,0:T(8,128)(2,1)}) %all-gather.4.cloned.1.call-update) | async-done | bytes 2097168 | tf_op jit(solution)/shard_map/all_gather | solution.py:59
  247.1 16.1 %convert_bitcast_fusion = bf16[16,64,128,64]{2,3,0,1:T(8,128)(2,1)} fusion(bf16[64,512,64,1]{2,1,3,0:T(8,128)(2,1)} %bitcast.54, bf16[16,512,128]{2,1,0:T(8,128)(2,1)} %all-gather.4.cloned.1.call-done), kind=kOutput, calls=%fused_computation.3 | convolution fusion | flops 8598323200 | bytes 23068672 | tf_op jit(solution)/shard_map/acq,pcd->padq/dot_general | solution.py:80
  263.2 30.3 %copy.98 = bf16[16,64,128,64]{3,2,1,0:T(8,128)(2,1)} copy(bf16[16,64,128,64]{2,3,0,1:T(8,128)(2,1)} %convert_bitcast_fusion) | data formatting | bytes 33554432 | tf_op jit(solution)/shard_map/convert_element_type | solution.py:82
  293.5 44.0 %reshape.110 = bf16[16,64,8192,1]{2,1,0,3:T(8,128)(2,1)} reshape(bf16[16,64,128,64]{3,2,1,0:T(8,128)(2,1)} %copy.98) | data formatting | bytes 33554432 | tf_op jit(solution)/shard_map/dot_general | solution.py:84
  337.6 12.2 %fusion = f32[16,64,4,64]{3,1,2,0:T(8,128)S(1)} fusion(bf16[4,64,8192,1]{2,1,0,3:T(8,128)(2,1)} %bitcast.59, bf16[16,64,8192,1]{2,1,0,3:T(8,128)(2,1)} %reshape.110), kind=kOutput, calls=%fused_computation.1 | convolution fusion | flops 4294967296 | bytes 22020096 | tf_op jit(solution)/shard_map/dot_general | solution.py:84
  350.1 0.1 constant_dynamic-slice_fusion
  350.3 2.7 copy.104
  353.0 2.5 reshape.96
  355.6 1.7 fusion.3
  357.4 30.0 %reduce-scatter.3.cloned.1.call-done = f32[16,64,128]{2,1,0:T(8,128)} async-done(((f32[16,64,512]{2,1,0:T(8,128)}), f32[16,64,128]{2,1,0:T(8,128)}) %reduce-scatter.3.cloned.1.call-update) | async-done | bytes 524304 | tf_op jit(solution)/shard_map/reduce_scatter | solution.py:98
  387.6 0.2 slice_reduce_fusion
  387.8 0.2 fusion.14
  388.1 64.9 %reduce-scatter.5.cloned.1.call-done = f32[2,64,128]{2,1,0:T(8,128)} async-done(((f32[16,64,128]{2,1,0:T(8,128)}), f32[2,64,128]{2,1,0:T(8,128)}) %reduce-scatter.5.cloned.1.call-update) | async-done | bytes 65552 | tf_op jit(solution)/shard_map/reduce_scatter | solution.py:99
  453.0 1.6 subtract_divide_fusion
  (46 shorter events, 1.2 us)
Async XLA Ops:
  6.5 1.6 copy-start
  6.5 196.2 %all-gather.6.cloned.1.call-start = ((), (), s32[]{:S(2)}) async-start(), calls=%async_computation.5 | async-start | bytes 10485760 | tf_op jit(solution)/shard_map/all_gather | solution.py:65
  31.9 32.2 %collective-permute-start.1 = (bf16[1,64,16,64]{3,0,2,1:T(2,128)(2,1)}, bf16[1,64,16,64]{3,0,2,1:T(2,128)(2,1)}, u32[]{:S(2)}, u32[]{:S(2)}) collective-permute-start(bf16[1,64,16,64]{3,0,2,1:T(2,128)(2,1)} %get-tuple-element.14), channel_id=1, source_target_pairs={{0,8},{4,12},{8,0},{12,4},{16,24},{20,28},{24,16},{28,20},{1,9},{5... | collective-permute-start | bytes 393224 | tf_op jit(solution)/shard_map/ppermute | solution.py:36
  39.8 13.4 %collective-permute-start = (bf16[1,64,16,64]{3,0,2,1:T(2,128)(2,1)S(1)}, bf16[1,64,16,64]{3,0,2,1:T(2,128)(2,1)S(1)}, u32[]{:S(2)}, u32[]{:S(2)}) collective-permute-start(bf16[1,64,16,64]{3,0,2,1:T(2,128)(2,1)S(1)} %get-tuple-element.19), channel_id=1, source_target_pairs={{0,4},{4,0},{8,12},{12,8},{16,20},{20,16},{24,28},{28,24},{1,5},{5... | collective-permute-start | bytes 393224 | tf_op jit(solution)/shard_map/ppermute | solution.py:36
  41.4 34.1 %collective-permute-start.2 = (bf16[1,64,16,64]{3,0,2,1:T(2,128)(2,1)}, bf16[1,64,16,64]{3,0,2,1:T(2,128)(2,1)S(1)}, u32[]{:S(2)}, u32[]{:S(2)}) collective-permute-start(bf16[1,64,16,64]{3,0,2,1:T(2,128)(2,1)} %get-tuple-element.15), channel_id=1, source_target_pairs={{0,12},{4,8},{8,4},{12,0},{16,28},{20,24},{24,20},{28,16},{1,13},{... | collective-permute-start | bytes 393224 | tf_op jit(solution)/shard_map/ppermute | solution.py:36
  41.4 34.1 %collective-permute-start.3 = (bf16[1,64,16,64]{3,0,2,1:T(2,128)(2,1)}, bf16[1,64,16,64]{3,0,2,1:T(2,128)(2,1)S(1)}, u32[]{:S(2)}, u32[]{:S(2)}) collective-permute-start(bf16[1,64,16,64]{3,0,2,1:T(2,128)(2,1)} %get-tuple-element.16), channel_id=1, source_target_pairs={{0,16},{4,20},{8,24},{12,28},{16,0},{20,4},{24,8},{28,12},{1,17},{... | collective-permute-start | bytes 393224 | tf_op jit(solution)/shard_map/ppermute | solution.py:36
  44.4 70.5 %collective-permute-start.4 = (bf16[1,64,16,64]{3,0,2,1:T(2,128)(2,1)}, bf16[1,64,16,64]{3,0,2,1:T(2,128)(2,1)S(1)}, u32[]{:S(2)}, u32[]{:S(2)}) collective-permute-start(bf16[1,64,16,64]{3,0,2,1:T(2,128)(2,1)} %get-tuple-element.17), channel_id=1, source_target_pairs={{0,20},{4,16},{8,28},{12,24},{16,4},{20,0},{24,12},{28,8},{1,21},{... | collective-permute-start | bytes 393224 | tf_op jit(solution)/shard_map/ppermute | solution.py:36
  53.3 61.7 %collective-permute-start.5 = (bf16[1,64,16,64]{3,0,2,1:T(2,128)(2,1)S(1)}, bf16[1,64,16,64]{3,0,2,1:T(2,128)(2,1)S(1)}, u32[]{:S(2)}, u32[]{:S(2)}) collective-permute-start(bf16[1,64,16,64]{3,0,2,1:T(2,128)(2,1)S(1)} %get-tuple-element.18), channel_id=1, source_target_pairs={{0,24},{4,28},{8,16},{12,20},{16,8},{20,12},{24,0},{28,4},{1,25},{... | collective-permute-start | bytes 393224 | tf_op jit(solution)/shard_map/ppermute | solution.py:36
  64.1 50.9 %collective-permute-start.6 = (bf16[1,64,16,64]{3,0,2,1:T(2,128)(2,1)S(1)}, bf16[1,64,16,64]{3,0,2,1:T(2,128)(2,1)S(1)}, u32[]{:S(2)}, u32[]{:S(2)}) collective-permute-start(bf16[1,64,16,64]{3,0,2,1:T(2,128)(2,1)S(1)} %get-tuple-element.13), channel_id=1, source_target_pairs={{0,28},{4,24},{8,20},{12,16},{16,12},{20,8},{24,4},{28,0},{1,29},{... | collective-permute-start | bytes 393224 | tf_op jit(solution)/shard_map/ppermute | solution.py:36
  117.3 129.8 %all-gather.4.cloned.1.call-start = ((), (), s32[]{:S(2)}) async-start(), calls=%async_computation.2 | async-start | bytes 2359296 | tf_op jit(solution)/shard_map/all_gather | solution.py:59
  118.0 269.4 %reduce-scatter.3.cloned.1.call-start = ((), (), s32[]{:S(2)}) async-start(), calls=%async_computation.3 | async-start | bytes 2621440 | tf_op jit(solution)/shard_map/reduce_scatter | solution.py:98
  129.1 46.1 %collective-permute-start.7 = (bf16[64,128,64]{1,2,0:T(8,128)(2,1)}, bf16[64,128,64]{1,2,0:T(8,128)(2,1)}, u32[]{:S(2)}, u32[]{:S(2)}) collective-permute-start(bf16[64,128,64]{1,2,0:T(8,128)(2,1)} %get-tuple-element.12), channel_id=1, source_target_pairs={{0,4},{4,8},{8,12},{12,0},{16,20},{20,24},{24,28},{28,16},{1,5},{5... | collective-permute-start | bytes 3145736 | tf_op jit(solution)/shard_map/ppermute | solution.py:78
  129.4 50.5 %collective-permute-start.8 = (bf16[64,128,64]{1,2,0:T(8,128)(2,1)}, bf16[64,128,64]{1,2,0:T(8,128)(2,1)}, u32[]{:S(2)}, u32[]{:S(2)}) collective-permute-start(bf16[64,128,64]{1,2,0:T(8,128)(2,1)} %get-tuple-element.11), channel_id=1, source_target_pairs={{0,8},{4,12},{8,0},{12,4},{16,24},{20,28},{24,16},{28,20},{1,9},{5... | collective-permute-start | bytes 3145736 | tf_op jit(solution)/shard_map/ppermute | solution.py:78
  151.4 43.1 %collective-permute-start.9 = (bf16[64,128,64]{1,2,0:T(8,128)(2,1)}, bf16[64,128,64]{1,2,0:T(8,128)(2,1)}, u32[]{:S(2)}, u32[]{:S(2)}) collective-permute-start(bf16[64,128,64]{1,2,0:T(8,128)(2,1)} %get-tuple-element.10), channel_id=1, source_target_pairs={{0,12},{4,0},{8,4},{12,8},{16,28},{20,16},{24,20},{28,24},{1,13},{... | collective-permute-start | bytes 3145736 | tf_op jit(solution)/shard_map/ppermute | solution.py:78
  355.6 99.0 %copy-start.1 = (bf16[64,64,256]{2,1,0:T(8,128)(2,1)S(1)}, bf16[64,64,256]{2,1,0:T(8,128)(2,1)}, u32[]{:S(2)}) copy-start(bf16[64,64,256]{2,1,0:T(8,128)(2,1)} %param.7) | copy-start | bytes 6291460
  357.3 30.2 %copy-start.4 = (f32[512]{0:T(512)S(1)}, f32[512]{0:T(512)}, u32[]{:S(2)}) copy-start(f32[512]{0:T(512)} %param.11) | copy-start | bytes 6148
  357.3 30.2 %copy-start.2 = (s32[2,2]{1,0:T(2,128)S(1)}, s32[2,2]{1,0:T(2,128)}, u32[]{:S(2)}) copy-start(s32[2,2]{1,0:T(2,128)} %param.9) | copy-start | bytes 52
  357.3 30.4 %copy-start.3 = (f32[128]{0:T(128)S(1)}, f32[128]{0:T(128)}, u32[]{:S(2)}) copy-start(f32[128]{0:T(128)} %param.10) | copy-start | bytes 1540
  357.3 30.7 %slice-start = ((f32[512]{0:T(512)}), f32[64]{0:T(128)S(1)}, s32[]{:S(2)}) async-start(f32[512]{0:T(512)} %param.11), calls=%async_computation.6 | async-start | bytes 1024 | tf_op jit(solution)/shard_map/slice | solution.py:109
  357.4 95.6 %reduce-scatter.5.cloned.1.call-start = ((), (), s32[]{:S(2)}) async-start(), calls=%async_computation.4 | async-start | bytes 589824 | tf_op jit(solution)/shard_map/reduce_scatter | solution.py:99
Sparse Core Ops, SparseCore 0:
  117.4 78.0 all-gather.5
  197.7 49.4 all-gather.3
  357.5 29.9 reduce-scatter.2
  391.0 61.9 reduce-scatter.4
